TPU v7x, 32 devices: a whole 2x2x4 slice. The times are simulated.
32 devices in a mesh: seq: 8 (over z, y), exp: 4 (over x, core).
Axes of the slice: x: 2, y: 2, z: 4, core: 2. Of those that a mesh axis runs over, the one named last changes fastest.
Arguments:
- hidden: bfloat16 [4, 1024, 2048], P('exp', 'seq'), may hold values from -6 to 6
- lengths: int32 [4, 4], P('exp'), may hold values from 1 to 512, 1024 in all within a row
- attn_gain: float32 [2048], replicated, may hold values from 0 to 10
- w_qkv: bfloat16 [2048, 3, 16, 128], P(None, None, 'seq'), may hold values from -0.125 to 0.125
- w_out: bfloat16 [16, 128, 2048], P('seq'), may hold values from -0.125 to 0.125
- moe_gain: float32 [2048], replicated, may hold values from 0.5 to 1.5
- router: bfloat16 [2048, 16], replicated, may hold values from -8 to 8
- routes: int32 [4, 1024, 6], P('exp', 'seq'), may hold values from 0 to 15, all different within a row; in each aligned block of 128 rows (0 to 127, 128 to 255, ..., all dimensions but the last counted through in order) at most 56 rows name the same one
- w_gate_up: bfloat16 [32, 2, 704, 2048], P(('seq', 'exp')), may hold values from -0.125 to 0.125
- w_down: bfloat16 [32, 704, 2048], P(('seq', 'exp')), may hold values from -0.15625 to 0.15625
- final_gain: float32 [2048], replicated, may hold values from 0.5 to 1.5
- lm_head: bfloat16 [102400, 2048], P(('seq', 'exp')), may hold values from -4 to 4
Outputs:
- layer_out: bfloat16 [4, 1024, 2048], P('exp', 'seq')
- logprobs: float32 [16, 102400], P(None, ('seq', 'exp'))
Inputs may be any that keep to these rules, and one draw needn't show every extreme that they name: `routes`: in the rows of one device no expert is named by more than 56 rows; in some devices one expert is named by exactly 56 rows. `lengths`: each row sums to 1024; its largest entry is 512.
All inputs are finite; a program needn't handle non-finite values.
Results may differ from a plain program's by a relative error of at most 0.0095.
The roundings to bfloat16 on the way count: a program that leaves them out, or rounds other values in their place, can miss the bound.
Values may be sent and summed in bfloat16 or wider, within the bound.
No kernel may reach another device: no remote copies, remote signals or barrier semaphores. Data moves between devices by JAX's collectives and lax.ppermute only.
A program may use at most 128 MiB of HBM per device.

v0:
```python
import jax
import jax.numpy as jnp
from jax import lax
from jax.sharding import PartitionSpec as P

epsilon = 1e-06


def joined(value, axis, join):
    pieces = jax.tree.map(lambda part: lax.all_gather(part, axis), value)
    head = jax.tree.map(lambda part: part[0], pieces)
    tail = jax.tree.map(lambda part: part[1:], pieces)
    subtotal, _ = lax.scan(lambda subtotal, piece: (join(subtotal, piece), None), head, tail)
    return subtotal


def rms_scale(values, gain):
    widened = values.astype(jnp.float32)
    inverse = lax.rsqrt(jnp.mean(widened * widened, axis=-1, keepdims=True) + epsilon)
    return widened * inverse * gain


def segment_layout(prompt_lengths, count):
    ends = jnp.cumsum(prompt_lengths)
    starts = ends - prompt_lengths
    places = jnp.arange(count, dtype=jnp.int32)
    member = ((places[:, None] >= starts[None, :]) & (places[:, None] < ends[None, :])).astype(
        jnp.int32
    )
    numbers = jnp.arange(prompt_lengths.shape[0], dtype=jnp.int32)
    segment = jnp.sum(member * numbers[None, :], axis=1)
    offset = places - jnp.sum(member * starts[None, :], axis=1)
    return (segment, offset)


def rotary(values, positions):
    half_size = values.shape[-1] // 2
    freqs = 10000.0 ** (-2.0 * jnp.arange(half_size, dtype=jnp.float32) / values.shape[-1])
    angles = positions.astype(jnp.float32)[:, None] * freqs[None, :]
    cosine = jnp.cos(angles)[:, None, :]
    sine = jnp.sin(angles)[:, None, :]
    first_half = values[..., :half_size]
    second_half = values[..., half_size:]
    return jnp.concatenate(
        [first_half * cosine - second_half * sine, second_half * cosine + first_half * sine],
        axis=-1,
    )


def merge_softmax(earlier, later):
    highest = jnp.maximum(earlier[0], later[0])
    return (
        highest,
        earlier[1] * jnp.exp(earlier[0] - highest) + later[1] * jnp.exp(later[0] - highest),
    )


def per_device(
    hidden,
    lengths,
    attn_gain,
    w_qkv,
    w_out,
    moe_gain,
    router,
    routes,
    w_gate_up,
    w_down,
    final_gain,
    lm_head,
):
    seq_count = lax.axis_size("seq")
    group_count = lax.axis_size("exp")
    device_count = seq_count * group_count
    token_rows = hidden[0]
    tok_rows = token_rows.shape[0]
    model_width = token_rows.shape[1]
    group_tokens = tok_rows * seq_count
    head_count = w_qkv.shape[2]
    head_size = w_qkv.shape[3]
    scale_factor = head_size ** (-0.5)
    prompt_lengths = lengths[0]
    segment, offset = segment_layout(prompt_lengths, group_tokens)
    normed = rms_scale(token_rows, attn_gain).astype(jnp.bfloat16)
    qkv_weight = w_qkv.reshape(model_width, 3 * head_count * head_size)
    qkv = jnp.dot(
        lax.all_gather(normed, "seq", axis=0, tiled=True),
        qkv_weight,
        preferred_element_type=jnp.float32,
    ).reshape(group_tokens, 3, head_count, head_size)
    query = rotary(qkv[:, 0], offset).astype(jnp.bfloat16)
    keys = rotary(qkv[:, 1], offset).astype(jnp.bfloat16)
    values = qkv[:, 2].astype(jnp.bfloat16)
    block_rows = min(512, group_tokens)
    key_places = jnp.arange(group_tokens, dtype=jnp.int32)

    def one_block(block_index):
        first_row = block_index * block_rows
        block_query = lax.dynamic_slice_in_dim(query, first_row, block_rows, 0)
        block_segment = lax.dynamic_slice_in_dim(segment, first_row, block_rows, 0)
        query_places = first_row + jnp.arange(block_rows, dtype=jnp.int32)
        scores = (
            jnp.einsum("qhd,khd->hqk", block_query, keys, preferred_element_type=jnp.float32)
            * scale_factor
        )
        allowed = (block_segment[:, None] == segment[None, :]) & (
            key_places[None, :] <= query_places[:, None]
        )
        scores = jnp.where(allowed[None], scores, -1e30)
        highest = jnp.max(scores, axis=2, keepdims=True)
        weights = jnp.exp(scores - highest)
        probs = (weights / jnp.sum(weights, axis=2, keepdims=True)).astype(jnp.bfloat16)
        return jnp.einsum("hqk,khd->qhd", probs, values, preferred_element_type=jnp.float32).astype(
            jnp.bfloat16
        )

    blocks = lax.map(one_block, jnp.arange(group_tokens // block_rows, dtype=jnp.int32))
    heads_flat = blocks.reshape(group_tokens, head_count * head_size)
    regrouped = lax.all_to_all(heads_flat, "seq", split_axis=0, concat_axis=1, tiled=True)
    full_weight = lax.all_gather(w_out, "seq", axis=0, tiled=True).reshape(-1, model_width)
    mixed = jnp.dot(regrouped, full_weight, preferred_element_type=jnp.float32)
    middle = (token_rows.astype(jnp.float32) + mixed).astype(jnp.bfloat16)
    expert_in = rms_scale(middle, moe_gain).astype(jnp.bfloat16)
    logits = jnp.dot(expert_in, router, preferred_element_type=jnp.float32)
    expert_count = router.shape[1]
    token_routes = routes[0]
    top_count = token_routes.shape[1]
    expert_ids = jnp.arange(expert_count, dtype=jnp.int32)
    chosen_mask = token_routes[:, :, None] == expert_ids[None, None, :]
    chosen = jnp.sum(jnp.where(chosen_mask, logits[:, None, :], 0.0), axis=2)
    gates = jax.nn.softmax(chosen, axis=-1)
    capacity = max(2, tok_rows * top_count * 7 // (6 * expert_count))
    flat_mask = chosen_mask.reshape(tok_rows * top_count, expert_count).astype(jnp.int32)
    earlier_count = jnp.cumsum(flat_mask, axis=0) - flat_mask
    slot_index = jnp.sum(earlier_count * flat_mask, axis=1)
    target = (token_routes.reshape(-1) * capacity + slot_index).reshape(tok_rows, top_count)
    slot_total = expert_count * capacity
    placed = target[:, :, None] == jnp.arange(slot_total, dtype=jnp.int32)[None, None, :]
    dispatch_table = jnp.any(placed, axis=1).astype(jnp.bfloat16)
    slot_weights = jnp.sum(jnp.where(placed, gates[:, :, None], 0.0), axis=1)
    packed = lax.dot_general(
        dispatch_table, expert_in, (((0,), (0,)), ((), ())), preferred_element_type=jnp.float32
    ).astype(jnp.bfloat16)
    shares = device_count // expert_count
    outgoing = jnp.broadcast_to(
        packed.reshape(expert_count, 1, capacity, model_width),
        (expert_count, shares, capacity, model_width),
    )
    outgoing = outgoing.reshape(device_count, capacity, model_width)
    gate_up = w_gate_up[0]
    down_weight = w_down[0]
    arrived = lax.all_to_all(outgoing, ("seq", "exp"), split_axis=0, concat_axis=0, tiled=True)
    arrived_shape = arrived.shape
    flat_rows = arrived.reshape(-1, model_width)
    both = jnp.einsum("rd,gfd->rgf", flat_rows, gate_up, preferred_element_type=jnp.float32)
    act = (jax.nn.silu(both[:, 0]) * both[:, 1]).astype(jnp.bfloat16)
    part = jnp.dot(act, down_weight, preferred_element_type=jnp.float32).astype(jnp.bfloat16)
    returned = lax.all_to_all(
        part.reshape(arrived_shape), ("seq", "exp"), split_axis=0, concat_axis=0, tiled=True
    )
    summed = jnp.sum(
        returned.reshape(expert_count, shares, capacity, model_width).astype(jnp.float32), axis=1
    )
    summed = summed.reshape(slot_total, model_width)
    routed = jnp.dot(
        slot_weights, summed, precision=lax.Precision.HIGHEST, preferred_element_type=jnp.float32
    )
    layer_rows = (middle.astype(jnp.float32) + routed).astype(jnp.bfloat16)
    prompt_count = prompt_lengths.shape[0]
    last_places = jnp.cumsum(prompt_lengths) - 1
    here_places = lax.axis_index("seq") * tok_rows + jnp.arange(tok_rows, dtype=jnp.int32)
    select_table = (last_places[:, None] == here_places[None, :]).astype(jnp.bfloat16)
    picked = jnp.dot(select_table, layer_rows, preferred_element_type=jnp.float32)
    board = jnp.zeros((group_count * prompt_count, model_width), jnp.float32)
    board = lax.dynamic_update_slice_in_dim(board, picked, lax.axis_index("exp") * prompt_count, 0)
    last_rows = lax.psum(board, ("seq", "exp"))
    final = rms_scale(last_rows, final_gain).astype(jnp.bfloat16)
    vocab_scores = lax.dot_general(
        final, lm_head, (((1,), (1,)), ((), ())), preferred_element_type=jnp.float32
    )
    local_peak = jnp.max(vocab_scores, axis=1)
    local_total = jnp.sum(jnp.exp(vocab_scores - local_peak[:, None]), axis=1)
    global_peak, global_total = joined((local_peak, local_total), ("seq", "exp"), merge_softmax)
    logprobs = vocab_scores - (global_peak + jnp.log(global_total))[:, None]
    return (layer_rows[None], logprobs)


def solution(mesh):
    return jax.shard_map(
        per_device,
        mesh=mesh,
        in_specs=(
            P("exp", "seq", None),
            P("exp", None),
            P(),
            P(None, None, "seq", None),
            P("seq", None, None),
            P(),
            P(),
            P("exp", "seq", None),
            P(("seq", "exp"), None, None, None),
            P(("seq", "exp"), None, None),
            P(),
            P(("seq", "exp"), None),
        ),
        out_specs=(P("exp", "seq", None), P(None, ("seq", "exp"))),
        check_vma=False,
    )
```

profile of v0, /device:TPU:0, one launch (start us, length us, event | category | flops | bytes accessed | tf_op | source)
XLA Modules:
  0.0 774.0 jit_solution(13950051054370654755)
XLA Ops:
  7.2 1.4 fusion.43
  8.6 2.0 fusion.45
  10.7 0.7 all-gather.7.cloned.1.call-update
  11.4 0.8 reduce-window.10
  12.3 8.1 %reshape.273 = bf16[2048,768]{1,0:T(8,128)(2,1)} reshape(bf16[2048,3,2,128]{3,2,1,0:T(2,128)(2,1)} %param.19) | data formatting | bytes 6291456 | tf_op jit(solution)/shard_map/reshape | solution.py:85
  20.3 4.8 copy.43
  25.3 1.0 multiply_cosine_fusion
  26.3 60.7 %all-gather.5.cloned.1.call-done = bf16[1024,2048]{1,0:T(8,128)(2,1)} async-done(((bf16[128,2048]{1,0:T(8,128)(2,1)}), bf16[1024,2048]{1,0:T(8,128)(2,1)}) %all-gather.5.cloned.1.call-update) | async-done | bytes 4194320 | tf_op jit(solution)/shard_map/all_gather | solution.py:87
  86.9 6.2 fusion.34
  93.6 1.3 pad_maximum_fusion
  95.0 1.1 copy.45
  96.0 1.3 fusion.46
  97.4 1.0 copy.46
  98.4 21.8 %while.24 = (s32[]{:T(128)}, bf16[2,512,2,128]{3,2,1,0:T(2,128)(2,1)}, s32[2]{0:T(128)S(1)}, s32[1024]{0:T(1024)S(1)}, bf16[1024,2,128]{0,2,1:T(8,128)(2,1)}, /*...) while((s32[]{:T(128)}, ...), condition=%wide.region_7.8_spmd.clone, body=%wide.region_4.7_spmd.clone.sunk | while | flops 544867840 | bytes 15751407 | solution.py:117
  100.2 4.9 fusion.96
  105.0 3.1 fusion.97
  108.5 0.8 copy-done.9
  111.1 4.9 fusion.96
  115.9 3.1 fusion.97
  119.4 0.8 copy-done.9
  120.2 2.3 all_to_all.20
  122.5 4.3 all-to-all-start
  127.8 3.2 reduce-window.11
  131.6 0.6 fusion.48
  132.2 0.9 copy.53
  133.6 11.9 %all-to-all-done = bf16[8,128,256]{2,1,0:T(8,128)(2,1)} async-done(((bf16[8,128,256]{2,1,0:T(8,128)(2,1)}), bf16[8,128,256]{2,1,0:T(8,128)(2,1)}, u32[]{:S(2)}, u32[]{:S(2)}) %all-to-all-start) | async-done | bytes 524320 | tf_op jit(solution)/shard_map/all_to_all | solution.py:119
  145.4 2.0 copy.48
  147.5 73.1 %all-gather.7.cloned.1.call-done = bf16[16,128,2048]{2,1,0:T(8,128)(2,1)} async-done(((bf16[2,128,2048]{2,1,0:T(8,128)(2,1)}), bf16[16,128,2048]{2,1,0:T(8,128)(2,1)}) %all-gather.7.cloned.1.call-update) | async-done | bytes 8388624 | tf_op jit(solution)/shard_map/all_gather | solution.py:120
  220.6 4.9 multiply_reduce_fusion
  225.5 3.0 convolution_convert_fusion.1
  228.5 3.2 broadcast_in_dim.59
  231.7 163.6 %all_to_all.29 = bf16[32,56,2048]{2,1,0:T(8,128)(2,1)S(1)} all-to-all(bf16[32,56,2048]{2,1,0:T(8,128)(2,1)S(1)} %bitcast.119), channel_id=1, replica_groups=mesh['seq'=8,'exp'=4] {'seq','exp'}, dimensions={0} | all-to-all | bytes 14680064 | tf_op jit(solution)/shard_map/all_to_all | solution.py:152
  395.3 12.7 %fusion.31 = f32[1792,2,704]{0,2,1:T(8,128)S(1)} fusion(bf16[1792,2048,1]{1,0,2:T(8,128)(2,1)S(1)} %bitcast.124, bf16[1,2,704,2048]{3,2,1,0:T(8,128)(2,1)} %param.24), kind=kOutput, calls=%fused_computation.33 | convolution fusion | flops 10334765056 | bytes 23199744 | tf_op jit(solution)/shard_map/rd,gfd->rgf/dot_general | solution.py:155
  408.1 8.2 %convolution_convert_fusion = bf16[1792,2048]{1,0:T(8,128)(2,1)} fusion(bf16[1,704,2048]{2,1,0:T(8,128)(2,1)S(1)} %copy-done, f32[1792,2,704]{0,2,1:T(8,128)S(1)} %fusion.31), kind=kOutput, calls=%fused_computation.32 | convolution fusion | flops 5178621952 | bytes 20316160 | tf_op jit(solution)/shard_map/dot_general | solution.py:157
  416.3 3.9 all-to-all-start.2
  420.6 1.5 fusion.63
  422.2 1.1 select_reduce_fusion
  423.3 160.0 %all-to-all-done.2 = bf16[32,56,2048]{2,1,0:T(8,128)(2,1)} async-done(((bf16[32,56,2048]{2,1,0:T(8,128)(2,1)}), bf16[32,56,2048]{2,1,0:T(8,128)(2,1)}, u32[]{:S(2)}, u32[]{:S(2)}) %all-to-all-start.2) | async-done | bytes 7340064 | tf_op jit(solution)/shard_map/all_to_all | solution.py:158
  583.4 5.5 convert_reduce_fusion
  588.9 4.2 fusion.42
  593.4 0.7 copy-done.10
  594.1 120.0 %all-reduce.5.cloned.1.call-done = f32[16,2048]{1,0:T(8,128)} async-done(((f32[16,2048]{1,0:T(8,128)}), f32[16,2048]{1,0:T(8,128)}) %all-reduce.5.cloned.1.call-update) | async-done | bytes 131088 | tf_op jit(solution)/shard_map/psum | solution.py:176
  714.1 1.0 multiply_reduce_fusion.1
  715.2 8.4 %fusion.70 = (f32[16]{0:T(128)S(1)}, f32[16,3200]{1,0:T(8,128)S(1)}) fusion(bf16[3200,2048]{1,0:T(8,128)(2,1)} %param.27, f32[16,2048]{1,0:T(8,128)} %all-reduce.5.cloned.1.call-done, f32[2048]{0:T(1024)S(1)} %copy-done.14, f32[16]{0:T(128)S(1)} %add_rsqrt_fusion), kind=kOutput, calls=%fused_computation.115 | convolution fusion | flops 209864688 | bytes 13451392 | tf_op jit(solution)/shard_map/dot_general | solution.py:178
  723.6 0.7 copy-done.6
  725.0 39.2 %all-reduce.2 = (f32[512]{0:T(512)S(1)}, f32[512]{0:T(512)S(1)}) all-reduce(f32[512]{0:T(512)S(1)} %dynamic-update-slice, f32[512]{0:T(512)S(1)} %dynamic-update-slice.1), channel_id=2, replica_groups=mesh['seq'=8,'exp'=4] {'seq','exp'}, use_global_device_ids=true, to_apply=%add | all-reduce | flops 1024 | bytes 8192
  764.4 1.3 while.23
  765.8 1.7 broadcast_subtract_fusion
  (123 shorter events, 8.3 us)
Async XLA Ops:
  7.2 400.9 %copy-start = (bf16[1,704,2048]{2,1,0:T(8,128)(2,1)S(1)}, bf16[1,704,2048]{2,1,0:T(8,128)(2,1)}, u32[]{:S(2)}) copy-start(bf16[1,704,2048]{2,1,0:T(8,128)(2,1)} %param.25) | copy-start | bytes 8650756
  7.2 79.7 %all-gather.5.cloned.1.call-start = ((), (), s32[]{:S(2)}) async-start(), calls=%async_computation.3 | async-start | bytes 4718592 | tf_op jit(solution)/shard_map/all_gather | solution.py:87
  10.7 209.9 %all-gather.7.cloned.1.call-start = ((), (), s32[]{:S(2)}) async-start(), calls=%async_computation.4 | async-start | bytes 9437184 | tf_op jit(solution)/shard_map/all_gather | solution.py:120
  12.3 12.9 %copy-start.15 = (s32[4,1]{0,1:T(1,128)}, s32[4,1]{0,1:T(1,128)S(1)}, u32[]{:S(2)}) copy-start(s32[4,1]{0,1:T(1,128)S(1)} %reduce-window.10) | copy-start | bytes 52
  20.3 4.8 copy-start.17
  93.1 1.9 copy-start.4
  98.4 28.4 %copy-start.13 = (s32[1,128,6]{1,0,2:T(1,128)S(1)}, s32[1,128,6]{1,0,2:T(1,128)}, u32[]{:S(2)}) copy-start(s32[1,128,6]{1,0,2:T(1,128)} %param.23) | copy-start | bytes 9220
  105.0 3.1 copy-start.8
  108.5 0.8 copy-start.9
  115.9 3.1 copy-start.8
  119.4 0.8 copy-start.9
  120.2 100.4 %copy-start.3 = (bf16[1,128,2048]{2,1,0:T(8,128)(2,1)S(1)}, bf16[1,128,2048]{2,1,0:T(8,128)(2,1)}, u32[]{:S(2)}) copy-start(bf16[1,128,2048]{2,1,0:T(8,128)(2,1)} %param.16) | copy-start | bytes 1572868
  122.5 23.0 %all-to-all-start = ((bf16[8,128,256]{2,1,0:T(8,128)(2,1)}), bf16[8,128,256]{2,1,0:T(8,128)(2,1)}, u32[]{:S(2)}, u32[]{:S(2)}) async-start(bf16[8,128,256]{2,1,0:T(8,128)(2,1)} %all_to_all.20), calls=%async_computation | async-start | bytes 1048576 | tf_op jit(solution)/shard_map/all_to_all | solution.py:119
  220.6 5.0 copy-start.12
  225.5 3.0 copy-start.1
  416.3 4.3 copy-start.16
  416.3 4.3 copy-start.11
  416.3 167.0 %all-to-all-start.2 = ((bf16[32,56,2048]{2,1,0:T(8,128)(2,1)}), bf16[32,56,2048]{2,1,0:T(8,128)(2,1)}, u32[]{:S(2)}, u32[]{:S(2)}) async-start(bf16[32,56,2048]{2,1,0:T(8,128)(2,1)} %bitcast.123), calls=%async_computation.2 | async-start | bytes 14680064 | tf_op jit(solution)/shard_map/all_to_all | solution.py:158
  420.3 293.9 %all-reduce.5.cloned.1.call-start = ((), (), s32[]{:S(2)}) async-start(), calls=%async_computation.5 | async-start | bytes 262144 | tf_op jit(solution)/shard_map/psum | solution.py:176
  583.4 5.5 copy-start.2
  583.4 5.5 copy-start.7
  588.9 126.3 %copy-start.14 = (f32[2048]{0:T(1024)S(1)}, f32[2048]{0:T(1024)}, u32[]{:S(2)}) copy-start(f32[2048]{0:T(1024)} %param.26) | copy-start | bytes 24580
  593.1 130.5 %copy-start.5 = (bf16[128,2048]{1,0:T(8,128)(2,1)}, bf16[128,2048]{1,0:T(8,128)(2,1)S(1)}, u32[]{:S(2)}) copy-start(bf16[128,2048]{1,0:T(8,128)(2,1)S(1)} %fusion.42) | copy-start | bytes 1572868
  593.4 0.7 copy-start.10
  723.6 0.7 copy-start.6
Sparse Core Ops, SparseCore 0:
  10.8 76.0 all-gather.4
  89.0 131.4 all-gather.6
  594.2 119.8 all-reduce.4
where the time goes:
time: 775 us; the launch traced here: 774 us
  waiting for transfers between devices  426 us (55%)
  blocking collectives  203 us (26%)
  matrix products  65.4 us (8%)
  local copies, waits for them, and re-layouts  31.1 us (4%)
  other arithmetic  23.9 us (3%)
  between operations  14.1 us (2%)
  starting transfers between devices  8.62 us (1%)
    all_to_all x1, blocking collectives, per_device(): lax.all_to_all(outgoing, ('seq', 'exp'), split_axis=0, concat_axis=0, til...  164 us
    all_to_all x1, waiting for transfers between devices, per_device(): lax.all_to_all(part.reshape(arrived_shape), ('seq', 'exp'), split_axis=0,...  160 us
    psum x1, waiting for transfers between devices, per_device(): last_rows = lax.psum(board, ('seq', 'exp'))  120 us
    all_gather x1, waiting for transfers between devices, per_device(): lax.all_gather(w_out, 'seq', axis=0, tiled=True).reshape(-1, model_width)  73.1 us
    all_gather x1, waiting for transfers between devices, per_device(): lax.all_gather(normed, 'seq', axis=0, tiled=True)  60.7 us
    unnamed x1, blocking collectives  39.2 us
  transfers between devices with their start and end apart: 5, of which 5 were waited for; matrix products, arithmetic and copies ran while one was open for 7% of the time, Pallas kernels for 0%

commit v1 on v0

--- a/solution.py
+++ b/solution.py
@@ -173,7 +173,9 @@
     picked = jnp.dot(select_table, layer_rows, preferred_element_type=jnp.float32)
     board = jnp.zeros((group_count * prompt_count, model_width), jnp.float32)
     board = lax.dynamic_update_slice_in_dim(board, picked, lax.axis_index("exp") * prompt_count, 0)
-    last_rows = lax.psum(board, ("seq", "exp"))
+    last_rows = board
+    for over in ("exp", "seq"):
+        last_rows = lax.psum(last_rows, over)
     final = rms_scale(last_rows, final_gain).astype(jnp.bfloat16)
     vocab_scores = lax.dot_general(
         final, lm_head, (((1,), (1,)), ((), ())), preferred_element_type=jnp.float32

time: 775 us -> 758 us (0.978)
  waiting for transfers between devices: 426 us -> 408 us
    psum x1 -> x2, waiting for transfers between devices: 120 us -> 102 us  [per_device(): last_rows = lax.psum(last_rows, over)]
  transfers between devices with their start and end apart: 5 -> 6, of which waited for: 5 -> 6; matrix products, arithmetic and copies ran while one was open for 7% -> 7% of each run, Pallas kernels for 0% -> 0%
where the time goes in v1:
time: 758 us; the launch traced here: 757 us
  waiting for transfers between devices  408 us (54%)
  blocking collectives  203 us (27%)
  matrix products  65.4 us (9%)
  local copies, waits for them, and re-layouts  31.1 us (4%)
  other arithmetic  23.9 us (3%)
  between operations  14.2 us (2%)
  starting transfers between devices  8.66 us (1%)
    all_to_all x1, blocking collectives, per_device(): lax.all_to_all(outgoing, ('seq', 'exp'), split_axis=0, concat_axis=0, til...  164 us
    all_to_all x1, waiting for transfers between devices, per_device(): lax.all_to_all(part.reshape(arrived_shape), ('seq', 'exp'), split_axis=0,...  160 us
    psum x2, waiting for transfers between devices, per_device(): last_rows = lax.psum(last_rows, over)  102 us
    all_gather x1, waiting for transfers between devices, per_device(): lax.all_gather(w_out, 'seq', axis=0, tiled=True).reshape(-1, model_width)  73.1 us
    all_gather x1, waiting for transfers between devices, per_device(): lax.all_gather(normed, 'seq', axis=0, tiled=True)  60.7 us
    unnamed x1, blocking collectives  39.6 us
  transfers between devices with their start and end apart: 6, of which 6 were waited for; matrix products, arithmetic and copies ran while one was open for 7% of the time, Pallas kernels for 0%

profile of v1, /device:TPU:0, one launch (start us, length us, event | category | flops | bytes accessed | tf_op | source)
XLA Modules:
  0.0 756.5 jit_solution(15383001745157966579)
XLA Ops:
  7.2 1.4 fusion.43
  8.6 2.0 fusion.45
  10.7 0.7 all-gather.7.cloned.1.call-update
  11.4 0.8 reduce-window.10
  12.3 8.1 %reshape.273 = bf16[2048,768]{1,0:T(8,128)(2,1)} reshape(bf16[2048,3,2,128]{3,2,1,0:T(2,128)(2,1)} %param.19) | data formatting | bytes 6291456 | tf_op jit(solution)/shard_map/reshape | solution.py:85
  20.3 4.8 copy.43
  25.3 1.0 multiply_cosine_fusion
  26.3 60.7 %all-gather.5.cloned.1.call-done = bf16[1024,2048]{1,0:T(8,128)(2,1)} async-done(((bf16[128,2048]{1,0:T(8,128)(2,1)}), bf16[1024,2048]{1,0:T(8,128)(2,1)}) %all-gather.5.cloned.1.call-update) | async-done | bytes 4194320 | tf_op jit(solution)/shard_map/all_gather | solution.py:87
  86.9 6.2 fusion.34
  93.6 1.3 pad_maximum_fusion
  95.0 1.1 copy.45
  96.0 1.3 fusion.46
  97.4 1.0 copy.46
  98.4 21.8 %while.24 = (s32[]{:T(128)}, bf16[2,512,2,128]{3,2,1,0:T(2,128)(2,1)}, s32[2]{0:T(128)S(1)}, s32[1024]{0:T(1024)S(1)}, bf16[1024,2,128]{0,2,1:T(8,128)(2,1)}, /*...) while((s32[]{:T(128)}, ...), condition=%wide.region_7.8_spmd.clone, body=%wide.region_4.7_spmd.clone.sunk | while | flops 544867840 | bytes 15751407 | solution.py:117
  100.2 4.9 fusion.96
  105.0 3.1 fusion.97
  108.5 0.8 copy-done.9
  111.1 4.9 fusion.96
  115.9 3.1 fusion.97
  119.4 0.8 copy-done.9
  120.2 2.3 all_to_all.20
  122.5 4.3 all-to-all-start
  127.8 3.2 reduce-window.11
  132.2 0.9 copy.53
  133.6 11.9 %all-to-all-done = bf16[8,128,256]{2,1,0:T(8,128)(2,1)} async-done(((bf16[8,128,256]{2,1,0:T(8,128)(2,1)}), bf16[8,128,256]{2,1,0:T(8,128)(2,1)}, u32[]{:S(2)}, u32[]{:S(2)}) %all-to-all-start) | async-done | bytes 524320 | tf_op jit(solution)/shard_map/all_to_all | solution.py:119
  145.4 2.0 copy.48
  147.5 73.1 %all-gather.7.cloned.1.call-done = bf16[16,128,2048]{2,1,0:T(8,128)(2,1)} async-done(((bf16[2,128,2048]{2,1,0:T(8,128)(2,1)}), bf16[16,128,2048]{2,1,0:T(8,128)(2,1)}) %all-gather.7.cloned.1.call-update) | async-done | bytes 8388624 | tf_op jit(solution)/shard_map/all_gather | solution.py:120
  220.6 4.9 multiply_reduce_fusion
  225.5 3.0 convolution_convert_fusion.1
  228.5 3.2 broadcast_in_dim.59
  231.7 163.6 %all_to_all.29 = bf16[32,56,2048]{2,1,0:T(8,128)(2,1)S(1)} all-to-all(bf16[32,56,2048]{2,1,0:T(8,128)(2,1)S(1)} %bitcast.119), channel_id=1, replica_groups=mesh['seq'=8,'exp'=4] {'seq','exp'}, dimensions={0} | all-to-all | bytes 14680064 | tf_op jit(solution)/shard_map/all_to_all | solution.py:152
  395.3 12.7 %fusion.31 = f32[1792,2,704]{0,2,1:T(8,128)S(1)} fusion(bf16[1792,2048,1]{1,0,2:T(8,128)(2,1)S(1)} %bitcast.124, bf16[1,2,704,2048]{3,2,1,0:T(8,128)(2,1)} %param.24), kind=kOutput, calls=%fused_computation.33 | convolution fusion | flops 10334765056 | bytes 23199744 | tf_op jit(solution)/shard_map/rd,gfd->rgf/dot_general | solution.py:155
  408.1 8.2 %convolution_convert_fusion = bf16[1792,2048]{1,0:T(8,128)(2,1)} fusion(bf16[1,704,2048]{2,1,0:T(8,128)(2,1)S(1)} %copy-done, f32[1792,2,704]{0,2,1:T(8,128)S(1)} %fusion.31), kind=kOutput, calls=%fused_computation.32 | convolution fusion | flops 5178621952 | bytes 20316160 | tf_op jit(solution)/shard_map/dot_general | solution.py:157
  416.3 3.9 all-to-all-start.2
  420.6 1.5 fusion.63
  422.2 1.1 select_reduce_fusion
  423.3 160.0 %all-to-all-done.2 = bf16[32,56,2048]{2,1,0:T(8,128)(2,1)} async-done(((bf16[32,56,2048]{2,1,0:T(8,128)(2,1)}), bf16[32,56,2048]{2,1,0:T(8,128)(2,1)}, u32[]{:S(2)}, u32[]{:S(2)}) %all-to-all-start.2) | async-done | bytes 7340064 | tf_op jit(solution)/shard_map/all_to_all | solution.py:158
  583.4 5.5 convert_reduce_fusion
  588.9 4.2 fusion.42
  593.4 0.7 copy-done.10
  594.1 28.9 %all-reduce.6.cloned.1.call-done = f32[16,2048]{1,0:T(8,128)} async-done(((f32[16,2048]{1,0:T(8,128)}), f32[16,2048]{1,0:T(8,128)}) %all-reduce.6.cloned.1.call-update) | async-done | bytes 131088 | tf_op jit(solution)/shard_map/psum | solution.py:178
  623.1 73.2 %all-reduce.8.cloned.1.call-done = f32[16,2048]{1,0:T(8,128)} async-done(((f32[16,2048]{1,0:T(8,128)}), f32[16,2048]{1,0:T(8,128)}) %all-reduce.8.cloned.1.call-update) | async-done | bytes 131088 | tf_op jit(solution)/shard_map/psum | solution.py:178
  696.3 1.0 multiply_reduce_fusion.1
  697.3 8.4 %fusion.70 = (f32[16]{0:T(128)S(1)}, f32[16,3200]{1,0:T(8,128)S(1)}) fusion(bf16[3200,2048]{1,0:T(8,128)(2,1)} %param.27, f32[16,2048]{1,0:T(8,128)} %all-reduce.8.cloned.1.call-done, f32[2048]{0:T(1024)S(1)} %copy-done.14, f32[16]{0:T(128)S(1)} %add_rsqrt_fusion), kind=kOutput, calls=%fused_computation.115 | convolution fusion | flops 209864688 | bytes 13451392 | tf_op jit(solution)/shard_map/dot_general | solution.py:180
  705.8 0.7 copy-done.6
  707.1 39.6 %all-reduce.2 = (f32[512]{0:T(512)S(1)}, f32[512]{0:T(512)S(1)}) all-reduce(f32[512]{0:T(512)S(1)} %dynamic-update-slice, f32[512]{0:T(512)S(1)} %dynamic-update-slice.1), channel_id=2, replica_groups=mesh['seq'=8,'exp'=4] {'seq','exp'}, use_global_device_ids=true, to_apply=%add | all-reduce | flops 1024 | bytes 8192
  747.0 1.3 while.23
  748.3 1.7 broadcast_subtract_fusion
  (126 shorter events, 9.0 us)
Async XLA Ops:
  7.2 400.9 %copy-start = (bf16[1,704,2048]{2,1,0:T(8,128)(2,1)S(1)}, bf16[1,704,2048]{2,1,0:T(8,128)(2,1)}, u32[]{:S(2)}) copy-start(bf16[1,704,2048]{2,1,0:T(8,128)(2,1)} %param.25) | copy-start | bytes 8650756
  7.2 79.7 %all-gather.5.cloned.1.call-start = ((), (), s32[]{:S(2)}) async-start(), calls=%async_computation.3 | async-start | bytes 4718592 | tf_op jit(solution)/shard_map/all_gather | solution.py:87
  10.7 209.9 %all-gather.7.cloned.1.call-start = ((), (), s32[]{:S(2)}) async-start(), calls=%async_computation.4 | async-start | bytes 9437184 | tf_op jit(solution)/shard_map/all_gather | solution.py:120
  12.3 12.9 %copy-start.15 = (s32[4,1]{0,1:T(1,128)}, s32[4,1]{0,1:T(1,128)S(1)}, u32[]{:S(2)}) copy-start(s32[4,1]{0,1:T(1,128)S(1)} %reduce-window.10) | copy-start | bytes 52
  20.3 4.8 copy-start.17
  93.1 1.9 copy-start.4
  98.4 28.4 %copy-start.13 = (s32[1,128,6]{1,0,2:T(1,128)S(1)}, s32[1,128,6]{1,0,2:T(1,128)}, u32[]{:S(2)}) copy-start(s32[1,128,6]{1,0,2:T(1,128)} %param.23) | copy-start | bytes 9220
  105.0 3.1 copy-start.8
  108.5 0.8 copy-start.9
  115.9 3.1 copy-start.8
  119.4 0.8 copy-start.9
  120.2 100.4 %copy-start.3 = (bf16[1,128,2048]{2,1,0:T(8,128)(2,1)S(1)}, bf16[1,128,2048]{2,1,0:T(8,128)(2,1)}, u32[]{:S(2)}) copy-start(bf16[1,128,2048]{2,1,0:T(8,128)(2,1)} %param.16) | copy-start | bytes 1572868
  122.5 23.0 %all-to-all-start = ((bf16[8,128,256]{2,1,0:T(8,128)(2,1)}), bf16[8,128,256]{2,1,0:T(8,128)(2,1)}, u32[]{:S(2)}, u32[]{:S(2)}) async-start(bf16[8,128,256]{2,1,0:T(8,128)(2,1)} %all_to_all.20), calls=%async_computation | async-start | bytes 1048576 | tf_op jit(solution)/shard_map/all_to_all | solution.py:119
  220.6 5.0 copy-start.12
  225.5 3.0 copy-start.1
  416.3 4.3 copy-start.16
  416.3 4.3 copy-start.11
  416.3 167.0 %all-to-all-start.2 = ((bf16[32,56,2048]{2,1,0:T(8,128)(2,1)}), bf16[32,56,2048]{2,1,0:T(8,128)(2,1)}, u32[]{:S(2)}, u32[]{:S(2)}) async-start(bf16[32,56,2048]{2,1,0:T(8,128)(2,1)} %bitcast.123), calls=%async_computation.2 | async-start | bytes 14680064 | tf_op jit(solution)/shard_map/all_to_all | solution.py:158
  420.3 202.8 %all-reduce.6.cloned.1.call-start = ((), (), s32[]{:S(2)}) async-start(), calls=%async_computation.5 | async-start | bytes 262144 | tf_op jit(solution)/shard_map/psum | solution.py:178
  583.4 5.5 copy-start.2
  583.4 5.5 copy-start.7
  588.9 108.4 %copy-start.14 = (f32[2048]{0:T(1024)S(1)}, f32[2048]{0:T(1024)}, u32[]{:S(2)}) copy-start(f32[2048]{0:T(1024)} %param.26) | copy-start | bytes 24580
  593.1 112.6 %copy-start.5 = (bf16[128,2048]{1,0:T(8,128)(2,1)}, bf16[128,2048]{1,0:T(8,128)(2,1)S(1)}, u32[]{:S(2)}) copy-start(bf16[128,2048]{1,0:T(8,128)(2,1)S(1)} %fusion.42) | copy-start | bytes 1572868
  593.4 0.7 copy-start.10
  594.1 102.2 %all-reduce.8.cloned.1.call-start = ((), (), s32[]{:S(2)}) async-start(), calls=%async_computation.6 | async-start | bytes 262144 | tf_op jit(solution)/shard_map/psum | solution.py:178
  705.7 0.7 copy-start.6
Sparse Core Ops, SparseCore 0:
  10.8 76.0 all-gather.4
  89.0 131.4 all-gather.6
  594.2 28.8 all-reduce.5
  626.6 69.5 all-reduce.7
